TPU v7x, 256 devices: a whole 4x4x8 slice. The times are simulated.
256 devices in a mesh: dp: 8 (over z_hi, x), ctx: 32 (over y, z_lo, core).
Axes of the slice: x: 4, y: 4, z: 8 (z_hi: 2, z_lo: 4; z = z_hi * 4 + z_lo), core: 2. Of those that a mesh axis runs over, the one named last changes fastest.
Arguments:
- y_first: bfloat16 [8, 4096, 1024], P('dp', 'ctx'), may hold values from -6 to 6
- x_second: bfloat16 [8, 4096, 1024], P('dp', 'ctx'), may hold values from -40 to 40
- grad_first: bfloat16 [8, 4096, 1024], P('dp', 'ctx'), may hold values from -6 to 6
- grad_second: bfloat16 [8, 4096, 1024], P('dp', 'ctx'), may hold values from -6 to 6
- w_query: bfloat16 [1024, 1024], P('dp'), may hold values from -0.1875 to 0.1875
- w_key: bfloat16 [1024, 1024], P('dp'), may hold values from -0.1875 to 0.1875
- w_value: bfloat16 [1024, 1024], P('dp'), may hold values from -0.1875 to 0.1875
- w_out: bfloat16 [1024, 1024], P('dp'), may hold values from -0.1875 to 0.1875
Outputs:
- x_first: bfloat16 [8, 4096, 1024], P('dp', 'ctx')
- grad_x_second: bfloat16 [8, 4096, 1024], P('dp', 'ctx')
- grad_query: float32 [1024, 1024], P(('dp', 'ctx'))
- grad_out: float32 [1024, 1024], P(('dp', 'ctx'))
All inputs are finite; a program needn't handle non-finite values.
Results may differ from a plain program's by a relative error of at most 0.012.
The roundings to bfloat16 on the way count: a program that leaves them out, or rounds other values in their place, can miss the bound.
Values may be sent and summed in bfloat16 or wider, within the bound.
No kernel may reach another device: no remote copies, remote signals or barrier semaphores. Data moves between devices by JAX's collectives and lax.ppermute only.
A program may use at most 128 MiB of HBM per device.

v0:
```python
import jax
import jax.numpy as jnp
from jax import lax
from jax.sharding import PartitionSpec as P

HEADS = 8
HEAD_DIM = 128


def prefix(shard, axis, combine, identity):
    size, here = (lax.axis_size(axis), lax.axis_index(axis))
    everything = lax.all_gather(shard, axis)
    start = jnp.broadcast_to(jnp.asarray(identity, shard.dtype), shard.shape)

    def turn(k, before):
        reached = k < here
        new = combine(before, everything[k])
        return jnp.where(reached, new, before)

    return lax.fori_loop(0, size, turn, start)


def carried_in(shard, axis, join, neutral):
    count = lax.axis_size(axis)
    place = lax.axis_index(axis)
    ahead = count - 1 - place
    gathered = lax.all_gather(shard.astype(jnp.bfloat16), axis)
    state = jnp.zeros_like(shard) + jnp.asarray(neutral, shard.dtype)

    def one(turn, state):
        source = count - 1 - turn
        return join(state, lax.dynamic_index_in_dim(gathered, source, 0, False).astype(shard.dtype))

    return lax.fori_loop(0, ahead, one, state)


def add_states(earlier, later):
    return earlier + later


def weight_grads(pairs, factor):
    width = pairs[0][0].shape[1]
    blocks = []
    for left, right in pairs:
        made = lax.dot_general(
            left, right, (((0,), (0,)), ((), ())), preferred_element_type=jnp.float32
        )
        blocks.append(factor * made)
    share = lax.psum_scatter(
        jnp.concatenate(blocks, 1), ("dp", "ctx"), scatter_dimension=0, tiled=True
    )
    return tuple((share[:, index * width : (index + 1) * width] for index in range(len(pairs))))


def on_device(y_first, x_second, grad_first, grad_second, w_query, w_key, w_value, w_out):
    batch, tokens_here, width = y_first.shape
    factor = float(batch * tokens_here * lax.axis_size("dp") * lax.axis_size("ctx")) ** (-0.5)
    full_query, full_key, full_value = (
        lax.all_gather(w_query, "dp", axis=0, tiled=True),
        lax.all_gather(w_key, "dp", axis=0, tiled=True),
        lax.all_gather(w_value, "dp", axis=0, tiled=True),
    )
    full_out = lax.all_gather(w_out, "dp", axis=0, tiled=True)
    second_wide = x_second.astype(jnp.float32)
    inv_rms = lax.rsqrt(jnp.mean(second_wide * second_wide, -1, keepdims=True) + 1e-06)
    normed_wide = second_wide * inv_rms
    normed = normed_wide.astype(jnp.bfloat16)

    def project(weight):
        made = jnp.einsum("btd,df->btf", normed, weight, preferred_element_type=jnp.float32)
        return made.astype(jnp.bfloat16).reshape(batch, tokens_here, HEADS, HEAD_DIM)

    queries = project(full_query)
    key_rows = project(full_key)
    values = project(full_value)
    local_state = jnp.einsum(
        "bthe,bthf->bhef", key_rows, values, preferred_element_type=jnp.float32
    )
    zeros_state = jnp.zeros_like(local_state)
    before = prefix(local_state, "ctx", add_states, zeros_state).astype(jnp.bfloat16)
    causal = jnp.tril(jnp.ones((tokens_here, tokens_here), dtype=bool))
    scores = jnp.einsum("bthe,bshe->bhts", queries, key_rows, preferred_element_type=jnp.float32)
    scores = jnp.where(causal[None, None], scores, 0.0).astype(jnp.bfloat16)
    mixed = jnp.einsum("bhts,bshf->bthf", scores, values, preferred_element_type=jnp.float32)
    mixed = mixed + jnp.einsum(
        "bthe,bhef->bthf", queries, before, preferred_element_type=jnp.float32
    )
    inv_head = lax.rsqrt(jnp.mean(mixed * mixed, -1, keepdims=True) + 1e-06)
    unit = mixed * inv_head
    attn_out = unit.astype(jnp.bfloat16).reshape(batch, tokens_here, width)
    attended = jnp.einsum("btf,fd->btd", attn_out, full_out, preferred_element_type=jnp.float32)
    x_first = (y_first.astype(jnp.float32) - attended).astype(jnp.bfloat16)
    grad_unit = jnp.einsum("btd,fd->btf", grad_first, full_out, preferred_element_type=jnp.float32)
    grad_unit = grad_unit.reshape(batch, tokens_here, HEADS, HEAD_DIM)
    grad_mixed = inv_head * (grad_unit - unit * jnp.mean(grad_unit * unit, -1, keepdims=True))
    grad_mixed = grad_mixed.astype(jnp.bfloat16)
    score_grad = jnp.einsum(
        "bthf,bshf->bhts", grad_mixed, values, preferred_element_type=jnp.float32
    )
    score_grad = jnp.where(causal[None, None], score_grad, 0.0).astype(jnp.bfloat16)
    grad_local = jnp.einsum(
        "bthe,bthf->bhef", queries, grad_mixed, preferred_element_type=jnp.float32
    )
    after_state = carried_in(grad_local, "ctx", add_states, zeros_state).astype(jnp.bfloat16)
    query_grad = jnp.einsum(
        "bhts,bshe->bthe", score_grad, key_rows, preferred_element_type=jnp.float32
    )
    query_grad = query_grad + jnp.einsum(
        "bthf,bhef->bthe", grad_mixed, before, preferred_element_type=jnp.float32
    )
    key_grad = jnp.einsum(
        "bhts,bthe->bshe", score_grad, queries, preferred_element_type=jnp.float32
    )
    key_grad = key_grad + jnp.einsum(
        "bshf,bhef->bshe", values, after_state, preferred_element_type=jnp.float32
    )
    value_grad = jnp.einsum(
        "bhts,bthf->bshf", scores, grad_mixed, preferred_element_type=jnp.float32
    )
    value_grad = value_grad + jnp.einsum(
        "bshe,bhef->bshf", key_rows, after_state, preferred_element_type=jnp.float32
    )
    query_grad = query_grad.astype(jnp.bfloat16).reshape(batch, tokens_here, width)
    key_grad = key_grad.astype(jnp.bfloat16).reshape(batch, tokens_here, width)
    value_grad = value_grad.astype(jnp.bfloat16).reshape(batch, tokens_here, width)
    grad_normed = jnp.einsum(
        "btf,df->btd", query_grad, full_query, preferred_element_type=jnp.float32
    )
    grad_normed = grad_normed + jnp.einsum(
        "btf,df->btd", key_grad, full_key, preferred_element_type=jnp.float32
    )
    grad_normed = grad_normed + jnp.einsum(
        "btf,df->btd", value_grad, full_value, preferred_element_type=jnp.float32
    )
    back = inv_rms * (
        grad_normed - normed_wide * jnp.mean(grad_normed * normed_wide, -1, keepdims=True)
    )
    grad_x_second = (grad_second.astype(jnp.float32) + back).astype(jnp.bfloat16)
    pairs = (
        (normed.reshape(-1, width), query_grad.reshape(-1, width)),
        (attn_out.reshape(-1, width), grad_first.reshape(-1, width)),
    )
    grad_query, grad_out = weight_grads(pairs, factor)
    return (x_first, grad_x_second, grad_query, grad_out)


def solution(mesh):
    placed = (
        P("dp", "ctx", None),
        P("dp", "ctx", None),
        P("dp", "ctx", None),
        P("dp", "ctx", None),
        P("dp", None),
        P("dp", None),
        P("dp", None),
        P("dp", None),
    )
    return jax.shard_map(
        on_device,
        mesh=mesh,
        in_specs=placed,
        out_specs=(
            P("dp", "ctx", None),
            P("dp", "ctx", None),
            P(("dp", "ctx"), None),
            P(("dp", "ctx"), None),
        ),
        check_vma=False,
    )
```

profile of v0, /device:TPU:1, one launch (start us, length us, event | category | flops | bytes accessed | tf_op | source)
XLA Modules:
  0.0 815.4 jit_solution(6239691303570350264)
XLA Ops:
  9.5 1.1 fusion.18
  10.6 77.0 %all-gather.13.cloned.1.call-done = bf16[1024,1024]{1,0:T(8,128)(2,1)} async-done(((bf16[128,1024]{1,0:T(8,128)(2,1)}), bf16[1024,1024]{1,0:T(8,128)(2,1)}) %all-gather.13.cloned.1.call-update) | async-done | bytes 2097168 | tf_op jit(solution)/shard_map/all_gather | solution.py:60
  87.5 2.2 convolution_convert_fusion.1
  90.0 71.8 %all-gather.9.cloned.1.call-done = bf16[1024,1024]{1,0:T(8,128)(2,1)} async-done(((bf16[128,1024]{1,0:T(8,128)(2,1)}), bf16[1024,1024]{1,0:T(8,128)(2,1)}) %all-gather.9.cloned.1.call-update) | async-done | bytes 2097168 | tf_op jit(solution)/shard_map/all_gather | solution.py:61
  161.8 2.1 fusion.9
  165.6 70.5 %all-gather.11.cloned.1.call-done = bf16[1024,1024]{1,0:T(8,128)(2,1)} async-done(((bf16[128,1024]{1,0:T(8,128)(2,1)}), bf16[1024,1024]{1,0:T(8,128)(2,1)}) %all-gather.11.cloned.1.call-update) | async-done | bytes 2097168 | tf_op jit(solution)/shard_map/all_gather | solution.py:59
  236.1 2.1 convolution_convert_fusion.2
  239.1 97.4 %all-gather.17.cloned.1.call-done = f32[256,128,128]{2,1,0:T(8,128)} async-done(((f32[8,128,128]{2,1,0:T(8,128)}), f32[256,128,128]{2,1,0:T(8,128)}) %all-gather.17.cloned.1.call-update) | async-done | bytes 16777232 | tf_op jit(solution)/shard_map/all_gather | solution.py:12
  336.5 40.0 %while.27 = (s32[]{:T(128)}, f32[1,8,128,128]{3,2,1,0:T(8,128)S(1)}, s32[]{:T(128)}, f32[32,1,8,128,128]{4,3,2,1,0:T(8,128)}, s32[]{:T(128)}, /*index=5*/s32[]{:T(128)}) while((s32[]{:T(128)}, f32[1,8,128,128]{3,2,1,0:T(8,128)S(1)}, s32[]{:T(128)}, f32[32,1,8,128,128]{4,3,2,1,0:T(8,128)}, s32[]{:T(128)}, /*index=5*/s32[]{:T(128)}) %tuple.88), condition=%wide.region_2.3_spmd.clone, body=%wide.region_1.2_spmd.clone.sunk | while | flops 393220 | bytes 1572965 | solution.py:20
  336.5 1.2 add_select_fusion.2
  337.7 1.2 add_select_fusion.2
  339.0 1.2 add_select_fusion.2
  340.2 1.2 add_select_fusion.2
  341.5 1.2 add_select_fusion.2
  342.7 1.2 add_select_fusion.2
  344.0 1.2 add_select_fusion.2
  345.2 1.2 add_select_fusion.2
  346.5 1.2 add_select_fusion.2
  347.7 1.2 add_select_fusion.2
  349.0 1.2 add_select_fusion.2
  350.2 1.2 add_select_fusion.2
  351.5 1.2 add_select_fusion.2
  352.8 1.2 add_select_fusion.2
  354.0 1.2 add_select_fusion.2
  355.3 1.2 add_select_fusion.2
  356.5 1.2 add_select_fusion.2
  357.8 1.2 add_select_fusion.2
  359.0 1.2 add_select_fusion.2
  360.3 1.2 add_select_fusion.2
  361.5 1.2 add_select_fusion.2
  362.8 1.2 add_select_fusion.2
  364.0 1.2 add_select_fusion.2
  365.3 1.2 add_select_fusion.2
  366.5 1.2 add_select_fusion.2
  367.8 1.2 add_select_fusion.2
  369.0 1.2 add_select_fusion.2
  370.3 1.2 add_select_fusion.2
  371.6 1.2 add_select_fusion.2
  372.8 1.2 add_select_fusion.2
  374.1 1.2 add_select_fusion.2
  375.3 1.2 add_select_fusion.2
  376.8 35.7 %all-gather.15.cloned.1.call-done = bf16[1024,1024]{1,0:T(8,128)(2,1)} async-done(((bf16[128,1024]{1,0:T(8,128)(2,1)}), bf16[1024,1024]{1,0:T(8,128)(2,1)}) %all-gather.15.cloned.1.call-update) | async-done | bytes 2097168 | tf_op jit(solution)/shard_map/all_gather | solution.py:63
  412.5 2.3 multiply_reduce_fusion
  418.1 4.1 pad_maximum_fusion
  424.4 2.1 fusion.53
  426.5 1.8 fusion.51
  428.3 1.2 fusion.5
  429.5 269.7 %all-reduce.3.cloned.1.call-done = f32[1024,2048]{0,1:T(8,128)} async-done(((f32[1024,2048]{0,1:T(8,128)}), f32[1024,2048]{0,1:T(8,128)}) %all-reduce.3.cloned.1.call-update) | async-done | bytes 8388624
  699.2 1.5 fusion.49
  702.3 68.8 %all-gather.19.cloned.1.call-done = bf16[256,128,128]{2,1,0:T(8,128)(2,1)} async-done(((bf16[8,128,128]{2,1,0:T(8,128)(2,1)}), bf16[256,128,128]{2,1,0:T(8,128)(2,1)}) %all-gather.19.cloned.1.call-update) | async-done | bytes 8388624 | tf_op jit(solution)/shard_map/all_gather | solution.py:27
  771.2 32.9 %while.26 = (s32[]{:T(128)}, f32[1,8,128,128]{3,2,1,0:T(8,128)S(1)}, s32[]{:T(128)}, bf16[32,1,8,128,128]{4,3,2,1,0:T(8,128)(2,1)}, s32[]{:T(128)}, /*index=5*/s32[]{:T(128)}, s32[]{:T(128)}, s32[]{:T(128)}) while((s32[]{:T(128)}, f32[1,8,128,128]{3,2,1,0:T(8,128)S(1)}, s32[]{:T(128)}, bf16[32,1,8,128,128]{4,3,2,1,0:T(8,128)(2,1)}, s32[]{:T(128)}, ...), condition=%wide.region_6.7_spmd, body=%wide.region_5.6_spmd.sunk | while | flops 262150 | bytes 1310863 | solution.py:34
  771.3 1.2 convert_add_fusion.2
  772.4 1.1 convert_add_fusion.2
  773.5 1.1 convert_add_fusion.2
  775.7 1.1 convert_add_fusion.2
  776.8 1.1 convert_add_fusion.2
  777.9 1.1 convert_add_fusion.2
  780.1 1.1 convert_add_fusion.2
  781.2 1.1 convert_add_fusion.2
  782.3 1.1 convert_add_fusion.2
  784.5 1.1 convert_add_fusion.2
  785.6 1.1 convert_add_fusion.2
  788.8 1.1 convert_add_fusion.2
  789.9 1.1 convert_add_fusion.2
  (98 shorter events, 34.8 us)
Async XLA Ops:
  7.2 405.4 %copy-start = (bf16[1,128,1024]{2,1,0:T(8,128)(2,1)S(1)}, bf16[1,128,1024]{2,1,0:T(8,128)(2,1)}, u32[]{:S(2)}) copy-start(bf16[1,128,1024]{2,1,0:T(8,128)(2,1)} %param.14) | copy-start | bytes 786436
  7.2 80.4 %all-gather.13.cloned.1.call-start = ((), (), s32[]{:S(2)}) async-start(), calls=%async_computation.2 | async-start | bytes 2359296 | tf_op jit(solution)/shard_map/all_gather | solution.py:60
  7.9 153.9 %all-gather.9.cloned.1.call-start = ((), (), s32[]{:S(2)}) async-start(), calls=%async_computation | async-start | bytes 2359296 | tf_op jit(solution)/shard_map/all_gather | solution.py:61
  8.7 153.2 %copy-start.2 = (bf16[1,128,1024]{2,1,0:T(8,128)(2,1)S(1)}, bf16[1,128,1024]{2,1,0:T(8,128)(2,1)}, u32[]{:S(2)}) copy-start(bf16[1,128,1024]{2,1,0:T(8,128)(2,1)} %param.13) | copy-start | bytes 786436
  8.7 227.4 %all-gather.11.cloned.1.call-start = ((), (), s32[]{:S(2)}) async-start(), calls=%async_computation.1 | async-start | bytes 2359296 | tf_op jit(solution)/shard_map/all_gather | solution.py:59
  9.4 327.1 %all-gather.17.cloned.1.call-start = ((), (), s32[]{:S(2)}) async-start(), calls=%async_computation.4 | async-start | bytes 17301504 | tf_op jit(solution)/shard_map/all_gather | solution.py:12
  89.7 148.7 %copy-start.10 = (bf16[128,1024]{1,0:T(8,128)(2,1)}, bf16[128,1024]{1,0:T(8,128)(2,1)S(1)}, u32[]{:S(2)}) copy-start(bf16[128,1024]{1,0:T(8,128)(2,1)S(1)} %convolution_convert_fusion.1) | copy-start | bytes 786436
  165.0 247.6 %all-gather.15.cloned.1.call-start = ((), (), s32[]{:S(2)}) async-start(), calls=%async_computation.3 | async-start | bytes 2359296 | tf_op jit(solution)/shard_map/all_gather | solution.py:63
  165.6 533.6 %all-reduce.3.cloned.1.call-start = ((), (), s32[]{:S(2)}) async-start(), calls=%async_computation.6 | async-start | bytes 16777216
  238.7 97.8 %copy-start.14 = (bf16[8,128,128]{2,1,0:T(8,128)(2,1)}, bf16[8,128,128]{2,1,0:T(8,128)(2,1)S(1)}, u32[]{:S(2)}) copy-start(bf16[8,128,128]{2,1,0:T(8,128)(2,1)S(1)} %fusion.3) | copy-start | bytes 786436
  415.0 2.3 copy-start.7
  415.4 0.7 copy-start.15
  416.6 5.7 copy-start.9
  422.2 1.1 copy-start.16
  422.3 4.3 copy-start.5
  422.3 348.9 %all-gather.19.cloned.1.call-start = ((), (), s32[]{:S(2)}) async-start(), calls=%async_computation.5 | async-start | bytes 8650752 | tf_op jit(solution)/shard_map/all_gather | solution.py:27
  424.4 3.9 copy-start.6
  424.4 3.9 copy-start.8
  424.4 3.9 copy-start.18
  771.2 32.9 %copy-start.12 = (f32[8,128,128]{2,1,0:T(8,128)S(1)}, f32[8,128,128]{2,1,0:T(8,128)}, u32[]{:S(2)}) copy-start(f32[8,128,128]{2,1,0:T(8,128)} %fusion.52) | copy-start | bytes 1572868
  771.2 33.2 %copy-start.11 = (bf16[128,1024]{1,0:T(8,128)(2,1)S(1)}, bf16[128,1024]{1,0:T(8,128)(2,1)}, u32[]{:S(2)}) copy-start(bf16[128,1024]{1,0:T(8,128)(2,1)} %copy-done.10) | copy-start | bytes 786436
  771.2 33.2 %copy-start.13 = (f32[8,128,128]{2,1,0:T(8,128)S(1)}, f32[8,128,128]{2,1,0:T(8,128)}, u32[]{:S(2)}) copy-start(f32[8,128,128]{2,1,0:T(8,128)} %fusion.53) | copy-start | bytes 1572868
  804.1 1.6 copy-start.3
  804.8 1.8 copy-start.4
  806.5 1.0 copy-start.17
  806.6 2.0 copy-start.1
Sparse Core Ops, SparseCore 0:
  10.6 76.8 all-gather.12
  90.2 71.6 all-gather.8
  164.5 71.6 all-gather.10
  237.8 98.6 all-gather.16
  339.0 73.5 all-gather.14
  422.4 276.7 all-reduce.2
  701.1 70.0 all-gather.18
where the time goes:
time: 818 us; the launch traced here: 815 us
  waiting for transfers between devices  694 us (85%)
  other arithmetic  77.8 us (10%)
  matrix products  22.5 us (3%)
  between operations  14.5 us (2%)
    unnamed x8, waiting for transfers between devices  272 us
    all_gather x1, waiting for transfers between devices, prefix(): everything = lax.all_gather(shard, axis)  97.4 us
    all_gather x1, waiting for transfers between devices, on_device(): lax.all_gather(w_key, 'dp', axis=0, tiled=True)  77 us
    all_gather x1, waiting for transfers between devices, on_device(): lax.all_gather(w_value, 'dp', axis=0, tiled=True)  71.8 us
    all_gather x1, waiting for transfers between devices, on_device(): lax.all_gather(w_query, 'dp', axis=0, tiled=True)  70.5 us
    all_gather x1, waiting for transfers between devices, carried_in(): gathered = lax.all_gather(shard.astype(jnp.bfloat16), axis)  68.8 us
    select_n x32, other arithmetic, turn(): return jnp.where(reached, new, before)  39.3 us
    all_gather x1, waiting for transfers between devices, on_device(): full_out = lax.all_gather(w_out, 'dp', axis=0, tiled=True)  35.7 us
  transfers between devices with their start and end apart: 7, of which 7 were waited for; matrix products, arithmetic and copies ran while one was open for 7% of the time, Pallas kernels for 0%

commit v1 on v0

--- a/solution.py
+++ b/solution.py
@@ -58,7 +58,9 @@
     full_query, full_key, full_value = (
         lax.all_gather(w_query, "dp", axis=0, tiled=True),
         lax.all_gather(w_key, "dp", axis=0, tiled=True),
-        lax.all_gather(w_value, "dp", axis=0, tiled=True),
+        jnp.concatenate(
+            lax.all_to_all(jnp.stack([w_value] * lax.axis_size("dp")), "dp", 0, 0), axis=0
+        ),
     )
     full_out = lax.all_gather(w_out, "dp", axis=0, tiled=True)
     second_wide = x_second.astype(jnp.float32)

time: 818 us -> 775 us (0.947)
  waiting for transfers between devices: 694 us -> 625 us
  starting transfers between devices: 0.27 us -> 11.8 us
    all_gather x1 -> x0, waiting for transfers between devices: 71.8 us -> none  [on_device(): lax.all_gather(w_value, 'dp', axis=0, tiled=True)]
    all_gather x1, waiting for transfers between devices: 77 us -> 94.1 us  [on_device(): lax.all_gather(w_key, 'dp', axis=0, tiled=True)]
    all_to_all x0 -> x1, starting transfers between devices: none -> 11.6 us  [on_device(): lax.all_to_all(jnp.stack([w_value] * lax.axis_size('dp')), 'dp', 0, 0)]
    unnamed x8 -> x7, waiting for transfers between devices: 272 us -> 269 us
  transfers between devices with their start and end apart: 7 -> 7, of which waited for: 7 -> 6; matrix products, arithmetic and copies ran while one was open for 7% -> 9% of each run, Pallas kernels for 0% -> 0%
where the time goes in v1:
time: 775 us; the launch traced here: 772 us
  waiting for transfers between devices  625 us (81%)
  other arithmetic  76.8 us (10%)
  matrix products  29.7 us (4%)
  between operations  14.5 us (2%)
  local copies, waits for them, and re-layouts  12.1 us (2%)
  starting transfers between devices  11.8 us (2%)
    unnamed x7, waiting for transfers between devices  269 us
    all_gather x1, waiting for transfers between devices, on_device(): lax.all_gather(w_key, 'dp', axis=0, tiled=True)  94.1 us
    all_gather x1, waiting for transfers between devices, prefix(): everything = lax.all_gather(shard, axis)  92.5 us
    all_gather x1, waiting for transfers between devices, on_device(): lax.all_gather(w_query, 'dp', axis=0, tiled=True)  68.3 us
    all_gather x1, waiting for transfers between devices, carried_in(): gathered = lax.all_gather(shard.astype(jnp.bfloat16), axis)  66.9 us
    select_n x32, other arithmetic, turn(): return jnp.where(reached, new, before)  39.3 us
    all_gather x1, waiting for transfers between devices, on_device(): full_out = lax.all_gather(w_out, 'dp', axis=0, tiled=True)  33.9 us
    add x30, other arithmetic, add_states(): return earlier + later  32.1 us
  transfers between devices with their start and end apart: 7, of which 6 were waited for; matrix products, arithmetic and copies ran while one was open for 9% of the time, Pallas kernels for 0%

profile of v1, /device:TPU:1, one launch (start us, length us, event | category | flops | bytes accessed | tf_op | source)
XLA Modules:
  0.0 771.5 jit_solution(11877163302674368486)
XLA Ops:
  7.9 2.6 stack.2
  10.5 11.6 %all-to-all-start = ((bf16[8,128,1024]{2,1,0:T(8,128)(2,1)}), bf16[8,128,1024]{2,1,0:T(8,128)(2,1)S(1)}, u32[]{:S(2)}, u32[]{:S(2)}) async-start(bf16[8,128,1024]{2,1,0:T(8,128)(2,1)} %stack.2), calls=%async_computation | async-start | bytes 4194304 | tf_op jit(solution)/shard_map/all_to_all | solution.py:62
  23.0 94.1 %all-gather.10.cloned.1.call-done = bf16[1024,1024]{1,0:T(8,128)(2,1)} async-done(((bf16[128,1024]{1,0:T(8,128)(2,1)}), bf16[1024,1024]{1,0:T(8,128)(2,1)}) %all-gather.10.cloned.1.call-update) | async-done | bytes 2097168 | tf_op jit(solution)/shard_map/all_gather | solution.py:60
  117.1 2.1 convolution_convert_fusion.1
  123.1 68.3 %all-gather.8.cloned.1.call-done = bf16[1024,1024]{1,0:T(8,128)(2,1)} async-done(((bf16[128,1024]{1,0:T(8,128)(2,1)}), bf16[1024,1024]{1,0:T(8,128)(2,1)}) %all-gather.8.cloned.1.call-update) | async-done | bytes 2097168 | tf_op jit(solution)/shard_map/all_gather | solution.py:59
  191.4 2.8 convolution_convert_fusion.2
  194.2 1.1 copy.61
  195.3 1.3 fusion.3
  197.3 2.1 fusion.23
  199.4 92.5 %all-gather.14.cloned.1.call-done = f32[256,128,128]{2,1,0:T(8,128)} async-done(((f32[8,128,128]{2,1,0:T(8,128)}), f32[256,128,128]{2,1,0:T(8,128)}) %all-gather.14.cloned.1.call-update) | async-done | bytes 16777232 | tf_op jit(solution)/shard_map/all_gather | solution.py:12
  291.9 40.0 %while.27 = (s32[]{:T(128)}, f32[1,8,128,128]{3,2,1,0:T(8,128)S(1)}, s32[]{:T(128)}, f32[32,1,8,128,128]{4,3,2,1,0:T(8,128)}, s32[]{:T(128)}, /*index=5*/s32[]{:T(128)}) while((s32[]{:T(128)}, f32[1,8,128,128]{3,2,1,0:T(8,128)S(1)}, s32[]{:T(128)}, f32[32,1,8,128,128]{4,3,2,1,0:T(8,128)}, s32[]{:T(128)}, /*index=5*/s32[]{:T(128)}) %tuple.86), condition=%wide.region_2.3_spmd.clone, body=%wide.region_1.2_spmd.clone.sunk | while | flops 393220 | bytes 1572965 | solution.py:20
  291.9 1.2 add_select_fusion.2
  293.2 1.2 add_select_fusion.2
  294.4 1.2 add_select_fusion.2
  295.7 1.2 add_select_fusion.2
  296.9 1.2 add_select_fusion.2
  298.2 1.2 add_select_fusion.2
  299.4 1.2 add_select_fusion.2
  300.7 1.2 add_select_fusion.2
  301.9 1.2 add_select_fusion.2
  303.2 1.2 add_select_fusion.2
  304.4 1.2 add_select_fusion.2
  305.7 1.2 add_select_fusion.2
  306.9 1.2 add_select_fusion.2
  308.2 1.2 add_select_fusion.2
  309.4 1.2 add_select_fusion.2
  310.7 1.2 add_select_fusion.2
  311.9 1.2 add_select_fusion.2
  313.2 1.2 add_select_fusion.2
  314.4 1.2 add_select_fusion.2
  315.7 1.2 add_select_fusion.2
  317.0 1.2 add_select_fusion.2
  318.2 1.2 add_select_fusion.2
  319.5 1.2 add_select_fusion.2
  320.7 1.2 add_select_fusion.2
  322.0 1.2 add_select_fusion.2
  323.2 1.2 add_select_fusion.2
  324.5 1.2 add_select_fusion.2
  325.7 1.2 add_select_fusion.2
  327.0 1.2 add_select_fusion.2
  328.2 1.2 add_select_fusion.2
  329.5 1.2 add_select_fusion.2
  330.7 1.2 add_select_fusion.2
  332.0 2.1 multiply_reduce_fusion.1
  334.1 33.9 %all-gather.12.cloned.1.call-done = bf16[1024,1024]{1,0:T(8,128)(2,1)} async-done(((bf16[128,1024]{1,0:T(8,128)(2,1)}), bf16[1024,1024]{1,0:T(8,128)(2,1)}) %all-gather.12.cloned.1.call-update) | async-done | bytes 2097168 | tf_op jit(solution)/shard_map/all_gather | solution.py:65
  368.0 2.5 multiply_reduce_fusion
  373.3 4.1 pad_maximum_fusion
  379.4 2.0 fusion.52
  382.4 3.2 fusion.51
  385.6 1.2 fusion.5
  386.8 267.5 %all-reduce.3.cloned.1.call-done = f32[1024,2048]{0,1:T(8,128)} async-done(((f32[1024,2048]{0,1:T(8,128)}), f32[1024,2048]{0,1:T(8,128)}) %all-reduce.3.cloned.1.call-update) | async-done | bytes 8388624
  654.3 2.3 fusion.49
  656.6 1.8 copy.52
  659.2 66.9 %all-gather.16.cloned.1.call-done = bf16[256,128,128]{2,1,0:T(8,128)(2,1)} async-done(((bf16[8,128,128]{2,1,0:T(8,128)(2,1)}), bf16[256,128,128]{2,1,0:T(8,128)(2,1)}) %all-gather.16.cloned.1.call-update) | async-done | bytes 8388624 | tf_op jit(solution)/shard_map/all_gather | solution.py:27
  726.2 32.8 %while.26 = (s32[]{:T(128)}, f32[1,8,128,128]{3,2,1,0:T(8,128)S(1)}, s32[]{:T(128)}, bf16[32,1,8,128,128]{4,3,2,1,0:T(8,128)(2,1)}, s32[]{:T(128)}, /*index=5*/s32[]{:T(128)}, s32[]{:T(128)}, s32[]{:T(128)}) while((s32[]{:T(128)}, f32[1,8,128,128]{3,2,1,0:T(8,128)S(1)}, s32[]{:T(128)}, bf16[32,1,8,128,128]{4,3,2,1,0:T(8,128)(2,1)}, s32[]{:T(128)}, ...), condition=%wide.region_6.7_spmd, body=%wide.region_5.6_spmd.sunk | while | flops 262150 | bytes 1310863 | solution.py:34
  726.2 1.1 convert_add_fusion.2
  727.3 1.1 convert_add_fusion.2
  728.4 1.1 convert_add_fusion.2
  730.6 1.1 convert_add_fusion.2
  731.7 1.1 convert_add_fusion.2
  732.8 1.1 convert_add_fusion.2
  735.0 1.1 convert_add_fusion.2
  759.0 1.5 fusion.7
  760.5 1.4 fusion.8
  (110 shorter events, 40.0 us)
Async XLA Ops:
  7.2 360.8 %copy-start = (bf16[1,128,1024]{2,1,0:T(8,128)(2,1)S(1)}, bf16[1,128,1024]{2,1,0:T(8,128)(2,1)}, u32[]{:S(2)}) copy-start(bf16[1,128,1024]{2,1,0:T(8,128)(2,1)} %param.14) | copy-start | bytes 786436
  7.2 109.9 %all-gather.10.cloned.1.call-start = ((), (), s32[]{:S(2)}) async-start(), calls=%async_computation.2 | async-start | bytes 2359296 | tf_op jit(solution)/shard_map/all_gather | solution.py:60
  10.5 12.4 %copy-start.2 = (bf16[1,128,1024]{2,1,0:T(8,128)(2,1)S(1)}, bf16[1,128,1024]{2,1,0:T(8,128)(2,1)}, u32[]{:S(2)}) copy-start(bf16[1,128,1024]{2,1,0:T(8,128)(2,1)} %param.13) | copy-start | bytes 786436
  10.5 109.6 %all-to-all-start = ((bf16[8,128,1024]{2,1,0:T(8,128)(2,1)}), bf16[8,128,1024]{2,1,0:T(8,128)(2,1)S(1)}, u32[]{:S(2)}, u32[]{:S(2)}) async-start(bf16[8,128,1024]{2,1,0:T(8,128)(2,1)} %stack.2), calls=%async_computation | async-start | bytes 4194304 | tf_op jit(solution)/shard_map/all_to_all | solution.py:62
  22.1 169.3 %all-gather.8.cloned.1.call-start = ((), (), s32[]{:S(2)}) async-start(), calls=%async_computation.1 | async-start | bytes 2359296 | tf_op jit(solution)/shard_map/all_gather | solution.py:59
  22.8 269.1 %all-gather.14.cloned.1.call-start = ((), (), s32[]{:S(2)}) async-start(), calls=%async_computation.4 | async-start | bytes 17301504 | tf_op jit(solution)/shard_map/all_gather | solution.py:12
  119.2 0.7 copy-start.17
  120.1 2.3 copy-start.11
  120.6 0.7 copy-start.8
  122.4 245.6 %all-gather.12.cloned.1.call-start = ((), (), s32[]{:S(2)}) async-start(), calls=%async_computation.3 | async-start | bytes 2359296 | tf_op jit(solution)/shard_map/all_gather | solution.py:65
  123.0 531.3 %all-reduce.3.cloned.1.call-start = ((), (), s32[]{:S(2)}) async-start(), calls=%async_computation.6 | async-start | bytes 16777216
  196.6 0.7 copy-start.20
  368.0 2.5 copy-start.5
  368.0 2.7 copy-start.9
  368.0 3.0 copy-start.12
  370.6 0.9 copy-start.6
  370.6 1.8 copy-start.13
  371.0 0.7 copy-start.22
  371.5 1.0 copy-start.15
  377.4 0.9 copy-start.7
  377.4 3.9 copy-start.21
  377.4 4.9 copy-start.16
  377.4 348.7 %all-gather.16.cloned.1.call-start = ((), (), s32[]{:S(2)}) async-start(), calls=%async_computation.5 | async-start | bytes 8650752 | tf_op jit(solution)/shard_map/all_gather | solution.py:27
  381.3 4.3 copy-start.4
  381.3 4.3 copy-start.14
  381.3 4.3 copy-start.24
  726.1 32.9 %copy-start.10 = (bf16[16,8,8,128]{3,2,1,0:T(8,128)(2,1)S(1)}, bf16[16,8,8,128]{3,2,1,0:T(8,128)(2,1)}, u32[]{:S(2)}) copy-start(bf16[16,8,8,128]{3,2,1,0:T(8,128)(2,1)} %copy-done.8) | copy-start | bytes 786436
  726.1 34.4 %copy-start.18 = (bf16[128,1024]{1,0:T(8,128)(2,1)S(1)}, bf16[128,1024]{1,0:T(8,128)(2,1)}, u32[]{:S(2)}) copy-start(bf16[128,1024]{1,0:T(8,128)(2,1)} %copy-done.17) | copy-start | bytes 786436
  759.0 2.9 copy-start.3
  759.0 2.9 copy-start.19
  762.7 1.0 copy-start.23
  762.8 1.9 copy-start.1
Sparse Core Ops, SparseCore 0:
  10.6 106.4 all-gather.9
  119.7 71.6 all-gather.7
  193.2 98.6 all-gather.13
  294.4 73.5 all-gather.11
  377.5 276.6 all-reduce.2
  656.0 70.0 all-gather.15
